TPU v7x, 32 devices: a whole 2x2x4 slice. The times are simulated.
32 devices in a mesh: space: 8 (over z, x), fsdp: 4 (over y, core).
Axes of the slice: x: 2, y: 2, z: 4, core: 2. Of those that a mesh axis runs over, the one named last changes fastest.
Arguments:
- features: bfloat16 [4, 128, 8, 8, 512], P('fsdp', 'space'), may hold values from -6 to 6
- cotangent: bfloat16 [4, 128, 8, 8, 512], P('fsdp', 'space'), may hold values from -6 to 6
- tissue: int32 [4, 128], P('fsdp', 'space'), may hold values 0 or 1
- weight: bfloat16 [27, 64, 64], P(None, 'fsdp'), may hold values from -0.15625 to 0.15625
Outputs:
- activations: bfloat16 [4, 128, 8, 8, 512], P('fsdp', 'space')
- input_grad: bfloat16 [4, 128, 8, 8, 512], P('fsdp', 'space')
- weight_grad: float32 [27, 64, 64], P(None, 'fsdp')
All inputs are finite; a program needn't handle non-finite values. No bound on the sum of `tissue` on one device may be relied on, other than what follows from the above.
Results may differ from a plain program's by a relative error of at most 0.0034.
Values may be sent and summed in bfloat16 or wider, within the bound.
No kernel may reach another device: no remote copies, remote signals or barrier semaphores. Data moves between devices by JAX's collectives and lax.ppermute only.
A program may use at most 192 MiB of HBM per device.

v0:
```python
import math
import jax
import jax.numpy as jnp
from jax import lax
from jax.sharding import PartitionSpec as P

BRICK_X = 2
BRICK_Y = 2
BRICK_Z = 4
PAIR = 2
DEPTH = 2
CONV_DIMS = ("NDHWC", "DHWIO", "NDHWC")


def from_behind(shard, axis, by):
    peers = lax.axis_size(axis)
    pairs = [(i, i + by) for i in range(peers) if 0 <= i + by < peers]
    return lax.ppermute(shard, axis, pairs)


def grid_shape(number):
    factors = [1, 1, 1]
    places = 0
    while number % 2 == 0:
        factors[places % 3] = factors[places % 3] * 2
        number = number // 2
        places = places + 1
    factors[0] = factors[0] * number
    return factors


def to_volume(bricks, edge_cells, lanes):
    per_brick = edge_cells // PAIR
    blocks = bricks.reshape(BRICK_X, BRICK_Y, BRICK_Z, edge_cells, edge_cells, per_brick, lanes)
    blocks = blocks.transpose(0, 3, 1, 4, 2, 5, 6)
    return blocks.reshape(BRICK_X * edge_cells, BRICK_Y * edge_cells, BRICK_Z * per_brick, lanes)


def to_bricks(volume, edge_cells, lanes):
    per_brick = edge_cells // PAIR
    blocks = volume.reshape(BRICK_X, edge_cells, BRICK_Y, edge_cells, BRICK_Z, per_brick, lanes)
    blocks = blocks.transpose(0, 2, 4, 1, 3, 5, 6)
    return blocks.reshape(BRICK_X * BRICK_Y * BRICK_Z, edge_cells, edge_cells, per_brick * lanes)


def neighbour_plane(portion, offset, present):
    arrived = from_behind(portion, "space", offset)
    return jnp.where(present, arrived, jnp.zeros_like(arrived))


def extend(volume, grid_dims, places, widths):
    strides = (grid_dims[1] * grid_dims[2], grid_dims[2], 1)
    for axis_pos in range(3):
        axis = axis_pos + 1
        extent = volume.shape[axis]
        width = widths[axis_pos]
        last_layer = lax.slice_in_dim(volume, extent - width, extent, axis=axis)
        first_layer = lax.slice_in_dim(volume, 0, width, axis=axis)
        from_below = neighbour_plane(last_layer, strides[axis_pos], places[axis_pos] > 0)
        from_above = neighbour_plane(
            first_layer, -strides[axis_pos], places[axis_pos] < grid_dims[axis_pos] - 1
        )
        volume = jnp.concatenate([from_below, volume, from_above], axis=axis)
    return volume


def super_kernel(weight_full, channels):
    taps = weight_full.reshape(3, 3, 3, channels, channels)
    zero = jnp.zeros((3, 3, channels, channels), weight_full.dtype)
    rows = []
    for dz in range(3):
        row = []
        for hi in range(PAIR):
            col = []
            for ho in range(PAIR):
                c = 2 * dz - 1 + hi - ho
                col.append(taps[:, :, c] if 0 <= c < 3 else zero)
            row.append(jnp.concatenate(col, axis=-1))
        rows.append(jnp.concatenate(row, axis=-2))
    return jnp.stack(rows, axis=2)


def fold_kernel_grad(grad_sup, channels):
    taps = [None, None, None]
    for dz in range(3):
        for hi in range(PAIR):
            for ho in range(PAIR):
                c = 2 * dz - 1 + hi - ho
                if 0 <= c < 3:
                    block = grad_sup[
                        :,
                        :,
                        dz,
                        hi * channels : (hi + 1) * channels,
                        ho * channels : (ho + 1) * channels,
                    ]
                    taps[c] = block if taps[c] is None else taps[c] + block
    return jnp.stack(taps, axis=2).reshape(27, channels, channels)


def conv(volume, kernel):
    return lax.conv_general_dilated(
        volume[None],
        kernel,
        (1, 1, 1),
        "VALID",
        dimension_numbers=CONV_DIMS,
        preferred_element_type=jnp.float32,
    )[0]


def kernel_grad(inputs, grads):
    out = lax.conv_general_dilated(
        inputs[None],
        grads[None],
        (1, 1, 1),
        "VALID",
        dimension_numbers=("CDHWN", "IDHWO", "NDHWC"),
        preferred_element_type=jnp.float32,
    )
    return out.transpose(1, 2, 3, 0, 4)


def local(features, cotangent, tissue, weight):
    edge_cells = features.shape[2]
    channels = weight.shape[2]
    lanes = PAIR * channels
    grid_dims = grid_shape(lax.axis_size("space"))
    index_now = lax.axis_index("space")
    places = (
        index_now // (grid_dims[1] * grid_dims[2]),
        index_now // grid_dims[2] % grid_dims[1],
        index_now % grid_dims[2],
    )
    weight_full = lax.all_gather(weight, "fsdp", axis=1, tiled=True)
    k_fwd = super_kernel(weight_full, channels)
    k_back = jnp.flip(k_fwd, (0, 1, 2)).transpose(0, 1, 2, 4, 3)
    present = tissue[0][:, None, None, None] > 0
    inputs = features[0]
    incoming = cotangent[0]
    masked = jnp.where(present, inputs, jnp.zeros_like(inputs))
    masked_cot = jnp.where(present, incoming, jnp.zeros_like(incoming))
    both = jnp.stack(
        [to_volume(masked, edge_cells, lanes), to_volume(masked_cot, edge_cells, lanes)]
    )
    grown = extend(both, grid_dims, places, (DEPTH, DEPTH, 1))
    grown = jnp.pad(grown, ((0, 0), (0, 0), (0, 0), (1, 1), (0, 0)))
    padded_in = grown[0]
    cot_ext = grown[1, 1:-1, 1:-1, 1:-1]
    pre_ext = conv(padded_in, k_fwd)
    gate_ext = jax.nn.sigmoid(pre_ext)
    slope_ext = gate_ext * (1.0 + pre_ext * (1.0 - gate_ext))
    grad_ext = (cot_ext.astype(jnp.float32) * slope_ext).astype(jnp.bfloat16)
    tissue_mask = tissue[0].astype(jnp.float32)[:, None, None, None]
    pre = to_bricks(pre_ext[1:-1, 1:-1, 1:-1], edge_cells, lanes)
    gate_val = to_bricks(gate_ext[1:-1, 1:-1, 1:-1], edge_cells, lanes)
    activations = (tissue_mask * (inputs.astype(jnp.float32) + pre * gate_val)).astype(jnp.bfloat16)
    back = to_bricks(conv(grad_ext, k_back), edge_cells, lanes)
    input_grad = (tissue_mask * (incoming.astype(jnp.float32) + back)).astype(jnp.bfloat16)
    total_cells = (
        lax.axis_size("space") * lax.axis_size("fsdp") * BRICK_X * BRICK_Y * BRICK_Z * edge_cells**3
    )
    grad_sup = kernel_grad(padded_in[1:-1, 1:-1, 1:-1], grad_ext[1:-1, 1:-1, 1:-1])
    grad_term = fold_kernel_grad(grad_sup, channels) / math.sqrt(total_cells)
    grad_part = lax.psum_scatter(grad_term, "fsdp", scatter_dimension=1, tiled=True)
    grad_part = lax.psum(grad_part, "space")
    return (activations[None], input_grad[None], grad_part)


def solution(mesh):
    return jax.shard_map(
        local,
        mesh=mesh,
        in_specs=(
            P("fsdp", "space", None, None, None),
            P("fsdp", "space", None, None, None),
            P("fsdp", "space"),
            P(None, "fsdp", None),
        ),
        out_specs=(
            P("fsdp", "space", None, None, None),
            P("fsdp", "space", None, None, None),
            P(None, "fsdp", None),
        ),
        check_vma=False,
    )
```

profile of v0, /device:TPU:0, one launch (start us, length us, event | category | flops | bytes accessed | tf_op | source)
XLA Modules:
  0.0 291.2 jit_solution(907447351510930595)
XLA Ops:
  12.0 6.7 %collective-permute-start = (bf16[2,2,16,16,128]{4,3,2,1,0:T(8,128)(2,1)S(1)}, bf16[2,2,16,16,128]{4,3,2,1,0:T(8,128)(2,1)S(1)}, u32[]{:S(2)}, u32[]{:S(2)}) collective-permute-start(bf16[2,2,16,16,128]{4,3,2,1,0:T(8,128)(2,1)S(1)} %get-tuple-element.11), channel_id=1, source_target_pairs={{0,16},{4,20},{8,24},{12,28},{1,17},{5,21},{9,25},{13,29},{2,18},{... | collective-permute-start | bytes 786440 | tf_op jit(solution)/shard_map/ppermute | solution.py:18
  18.7 7.7 %all_gather.3 = bf16[27,64,64]{2,1,0:T(8,128)(2,1)S(1)} all-gather(bf16[27,16,64]{2,1,0:T(8,128)(2,1)S(1)} %copy-done.14), channel_id=1, replica_groups=mesh['space'=8,'fsdp'=4] {'fsdp'}, dimensions={1}, use_global_device_ids=true | all-gather | bytes 276480 | tf_op jit(solution)/shard_map/all_gather | solution.py:135
  30.6 4.8 %collective-permute-start.2 = (bf16[2,20,2,16,128]{4,3,2,1,0:T(8,128)(2,1)S(1)}, bf16[2,20,2,16,128]{4,3,2,1,0:T(8,128)(2,1)S(1)}, u32[]{:S(2)}, u32[]{:S(2)}) collective-permute-start(bf16[2,20,2,16,128]{4,3,2,1,0:T(8,128)(2,1)S(1)} %get-tuple-element.9), channel_id=1, source_target_pairs={{0,8},{4,12},{8,16},{12,20},{16,24},{20,28},{1,9},{5,13},{9,17},{1... | collective-permute-start | bytes 983048 | tf_op jit(solution)/shard_map/ppermute | solution.py:18
  35.7 5.6 %collective-permute-done.3 = bf16[2,20,2,16,128]{4,3,2,1,0:T(8,128)(2,1)S(1)} collective-permute-done((bf16[2,20,2,16,128]{4,3,2,1,0:T(8,128)(2,1)S(1)}, bf16[2,20,2,16,128]{4,3,2,1,0:T(8,128)(2,1)S(1)}, u32[]{:S(2)}, u32[]{:S(2)}) %collective-permute-start.3) | collective-permute-done | bytes 327712 | tf_op jit(solution)/shard_map/ppermute | solution.py:18
  46.2 4.7 %collective-permute-start.4 = (bf16[2,20,20,1,128]{4,3,2,1,0:T(2,128)(2,1)S(1)}, bf16[2,20,20,1,128]{4,3,2,1,0:T(2,128)(2,1)S(1)}, u32[]{:S(2)}, u32[]{:S(2)}) collective-permute-start(bf16[2,20,20,1,128]{4,3,2,1,0:T(2,128)(2,1)S(1)} %get-tuple-element.7), channel_id=1, source_target_pairs={{0,4},{4,8},{8,12},{12,16},{16,20},{20,24},{24,28},{1,5},{5,9},{9,... | collective-permute-start | bytes 614408 | tf_op jit(solution)/shard_map/ppermute | solution.py:18
  50.9 6.3 %collective-permute-done.5 = bf16[2,20,20,1,128]{4,3,2,1,0:T(2,128)(2,1)S(1)} collective-permute-done((bf16[2,20,20,1,128]{4,3,2,1,0:T(2,128)(2,1)S(1)}, bf16[2,20,20,1,128]{4,3,2,1,0:T(2,128)(2,1)S(1)}, u32[]{:S(2)}, u32[]{:S(2)}) %collective-permute-start.5) | collective-permute-done | bytes 204832 | tf_op jit(solution)/shard_map/ppermute | solution.py:18
  57.7 8.5 %collective-permute-done.4 = bf16[2,20,20,1,128]{4,3,2,1,0:T(2,128)(2,1)S(1)} collective-permute-done((bf16[2,20,20,1,128]{4,3,2,1,0:T(2,128)(2,1)S(1)}, bf16[2,20,20,1,128]{4,3,2,1,0:T(2,128)(2,1)S(1)}, u32[]{:S(2)}, u32[]{:S(2)}) %collective-permute-start.4) | collective-permute-done | bytes 204832 | tf_op jit(solution)/shard_map/ppermute | solution.py:18
  66.6 5.9 %pad_maximum_fusion = bf16[2,20,20,18,128]{4,3,2,1,0:T(8,128)(2,1)S(1)} fusion(bf16[2,20,20,1,128]{4,3,2,1,0:T(2,128)(2,1)S(1)} %broadcast_select_fusion.1, bf16[2,20,2,16,128]{4,3,2,1,0:T(8,128)(2,1)S(1)} %broadcast_select_fusion.3, bf16[2,2,16,16,128]{4,3,2,1,0:T(8,128)(2,1)S(1)} %broadcast_select_fusion.5, bf16[1,16,16,16,128]{4,3,2,1,0:T(8,128)(2,1)S(1)} %bitcast.89, ...), kind=kLoop, calls=%fused_computation.6 | loop fusion | flops 29491200 | bytes 7372800 | tf_op jit(solution)/shard_map/concatenate | solution.py:63
  72.5 3.0 %fusion.29 = (bf16[20,20,20,128]{3,2,1,0:T(8,128)(2,1)}, bf16[20,20,1,20,128]{4,3,1,0,2:T(8,128)(2,1)S(1)}) fusion(bf16[2,20,20,18,128]{4,3,2,1,0:T(8,128)(2,1)S(1)} %pad_maximum_fusion), kind=kLoop, calls=%fused_computation.39 | loop fusion | bytes 7782400 | tf_op jit(solution)/shard_map/squeeze | solution.py:148
  77.5 17.0 %add_multiply_fusion = (f32[18,18,8,3,128]{4,2,3,1,0:T(8,128)}, f32[18,18,8,3,128]{4,2,3,1,0:T(8,128)S(1)}) fusion(bf16[3,3,1,128,128]{4,3,2,1,0:T(8,128)(2,1)S(1)} %get-tuple-element.21, bf16[3,3,1,128,128]{4,3,2,1,0:T(8,128)(2,1)S(1)} %get-tuple-element.20, bf16[3,3,1,128,128]{4,3,2,1,0:T(8,128)(2,1)S(1)} %get-tuple-element.19, ...), kind=kOutput, calls=%fused_computation.17 | convolution fusion | flops 6900842496 | bytes 12738584 | tf_op jit(solution)/shard_map/conv_general_dilated | solution.py:102
  94.4 4.0 %copy.40 = f32[18,18,8,3,128]{4,3,2,1,0:T(4,128)} copy(f32[18,18,8,3,128]{4,2,3,1,0:T(8,128)S(1)} %get-tuple-element.27) | data formatting | bytes 7962624 | tf_op jit(solution)/shard_map/conv_general_dilated | solution.py:102
  98.4 7.3 %reshape.72 = f32[18,18,1,24,128]{4,3,1,0,2:T(8,128)} reshape(f32[18,18,8,3,128]{4,3,2,1,0:T(4,128)} %copy.40) | data formatting | bytes 7962624 | tf_op jit(solution)/shard_map/conv_general_dilated | solution.py:102
  105.7 4.5 %slice_bitcast_fusion.1 = f32[18,18,18,128]{3,2,1,0:T(8,128)} fusion(f32[18,18,1,24,128]{4,3,1,0,2:T(8,128)} %reshape.72), kind=kLoop, calls=%fused_computation.16 | loop fusion | bytes 5971968 | tf_op jit(solution)/shard_map/squeeze | solution.py:102
  113.2 3.9 %convert_bitcast_fusion = f32[18,18,18,128]{3,2,1,0:T(8,128)} fusion(bf16[2,20,20,18,128]{4,3,2,1,0:T(8,128)(2,1)} %copy-done), kind=kLoop, calls=%fused_computation.4 | loop fusion | flops 746496 | bytes 4478976 | tf_op jit(solution)/shard_map/convert_element_type | solution.py:153
  117.1 4.0 %copy.42 = f32[18,18,8,3,128]{4,3,2,1,0:T(4,128)} copy(f32[18,18,8,3,128]{4,2,3,1,0:T(8,128)S(1)} %copy-done.9) | data formatting | bytes 7962624 | tf_op jit(solution)/shard_map/mul | solution.py:152
  121.0 7.3 %reshape.81 = f32[18,18,1,24,128]{4,3,1,0,2:T(8,128)} reshape(f32[18,18,8,3,128]{4,3,2,1,0:T(4,128)} %copy.42) | data formatting | bytes 7962624 | tf_op jit(solution)/shard_map/mul | solution.py:152
  128.3 3.2 %fusion.22 = bf16[18,18,1,18,128]{4,3,1,0,2:T(8,128)(2,1)S(1)} fusion(f32[18,18,1,24,128]{4,3,1,0,2:T(8,128)} %reshape.81, bf16[2,20,20,18,128]{4,3,2,1,0:T(8,128)(2,1)} %copy-done), kind=kLoop, calls=%fused_computation.33 | loop fusion | flops 2239488 | bytes 5971968 | tf_op jit(solution)/shard_map/convert_element_type | solution.py:153
  133.1 5.5 %reshape.75 = bf16[18,18,1,8,3,128]{5,4,3,1,0,2:T(4,128)(2,1)S(1)} reshape(bf16[18,18,1,24,128]{4,3,1,0,2:T(8,128)(2,1)} %pad.11) | data formatting | bytes 3981312 | tf_op jit(solution)/shard_map/conv_general_dilated | solution.py:102
  144.1 4.3 %fusion.31 = (bf16[1,16,16,16,128]{4,3,2,1,0:T(8,128)(2,1)S(1)}, f32[16,16,16,128]{3,2,1,0:T(8,128)}) fusion(f32[18,18,18,128]{3,2,1,0:T(8,128)S(1)} %copy-done.2, f32[18,18,18,128]{3,2,1,0:T(8,128)S(1)} %copy-done.3, f32[18,18,18,128]{3,2,1,0:T(8,128)} %convert_bitcast_fusion), kind=kLoop, calls=%fused_computation.41 | loop fusion | flops 3670016 | bytes 9437184 | tf_op jit(solution)/shard_map/broadcast_in_dim | solution.py:115
  148.4 32.2 %fusion.17 = f32[3,3,3,128,128]{4,3,2,1,0:T(8,128)S(1)} fusion(bf16[1,18,18,18,128]{4,3,2,1,0:T(8,128)(2,1)S(1)} %slice_bitcast_fusion.2, bf16[1,16,16,16,128]{4,3,2,1,0:T(8,128)(2,1)S(1)} %get-tuple-element.3), kind=kOutput, calls=%fused_computation.25 | convolution fusion | flops 3623878656 | bytes 4311040 | tf_op jit(solution)/shard_map/transpose | solution.py:121
  182.9 13.3 %fusion.25 = f32[16,16,8,3,128]{4,2,3,1,0:T(8,128)S(1)} fusion(bf16[18,18,1,7,2,128]{5,3,4,1,0,2:T(8,128)(2,1)S(1)} %copy-done.10, bf16[18,18,1,8,3,128]{5,3,4,1,0,2:T(8,128)(2,1)S(1)} %copy-done.7, pred[8,3]{0,1:T(4,128)(4,1)S(1)} %copy-done.17, bf16[3,3,1,128,128]{4,3,2,1,0:T(8,128)(2,1)} %copy-done.13, bf16[3,3,1,128,128]{4,3,2,1,0:T(8,128)(2,1)} %copy-done.12, ...), kind=kOutput, calls=%fused_computation.37 | convolution fusion | flops 5447442432 | bytes 7182360 | tf_op jit(solution)/shard_map/conv_general_dilated | solution.py:102
  200.4 7.6 %reduce-scatter.2.cloned.1.call-done = f32[27,16,64]{2,1,0:T(8,128)} async-done(((f32[27,64,64]{2,1,0:T(8,128)}), f32[27,16,64]{2,1,0:T(8,128)}) %reduce-scatter.2.cloned.1.call-update) | async-done | bytes 110608 | tf_op jit(solution)/shard_map/reduce_scatter | solution.py:165
  208.1 4.2 %multiply_convert_fusion = (bf16[1,16,8,8,512]{4,3,2,1,0:T(8,128)(2,1)}, bf16[1,16,8,8,512]{4,3,2,1,0:T(8,128)(2,1)}) fusion(f32[1,16,8,8,512]{4,3,2,1,0:T(8,128)S(1)} %bitcast.94, bf16[1,16,8,8,512]{4,3,2,1,0:T(8,128)(2,1)} %param.5, f32[16]{0:T(128)S(1)} %copy-done.15, f32[1,16,8,8,512]{4,3,2,1,0:T(8,128)} %bitcast.95, ...), kind=kLoop, calls=%fused_computation.29 | loop fusion | flops 4194304 | bytes 8388672 | tf_op jit(solution)/shard_map/convert_element_type | solution.py:159
  212.3 70.0 %all-reduce.7.cloned.1.call-done = f32[27,16,64]{2,1,0:T(8,128)} async-done(((f32[27,16,64]{2,1,0:T(8,128)}), f32[27,16,64]{2,1,0:T(8,128)}) %all-reduce.7.cloned.1.call-update) | async-done | bytes 110608 | tf_op jit(solution)/shard_map/psum | solution.py:166
  (79 shorter events, 35.0 us)
Async XLA Ops:
  7.2 11.5 %copy-start.14 = (bf16[27,16,64]{2,1,0:T(8,128)(2,1)S(1)}, bf16[27,16,64]{2,1,0:T(8,128)(2,1)}, u32[]{:S(2)}) copy-start(bf16[27,16,64]{2,1,0:T(8,128)(2,1)} %param.7) | copy-start | bytes 165892
  7.2 200.8 %reduce-scatter.2.cloned.1.call-start = ((), (), s32[]{:S(2)}) async-start(), calls=%async_computation.1 | async-start | bytes 1105920 | tf_op jit(solution)/shard_map/reduce_scatter | solution.py:165
  10.7 17.4 %collective-permute-start.1 = (bf16[2,2,16,16,128]{4,3,2,1,0:T(8,128)(2,1)S(1)}, bf16[2,2,16,16,128]{4,3,2,1,0:T(8,128)(2,1)}, u32[]{:S(2)}, u32[]{:S(2)}) collective-permute-start(bf16[2,2,16,16,128]{4,3,2,1,0:T(8,128)(2,1)S(1)} %get-tuple-element.12), channel_id=1, source_target_pairs={{16,0},{20,4},{24,8},{28,12},{17,1},{21,5},{25,9},{29,13},{18,2},{... | collective-permute-start | bytes 786440 | tf_op jit(solution)/shard_map/ppermute | solution.py:18
  12.0 17.0 %collective-permute-start = (bf16[2,2,16,16,128]{4,3,2,1,0:T(8,128)(2,1)S(1)}, bf16[2,2,16,16,128]{4,3,2,1,0:T(8,128)(2,1)S(1)}, u32[]{:S(2)}, u32[]{:S(2)}) collective-permute-start(bf16[2,2,16,16,128]{4,3,2,1,0:T(8,128)(2,1)S(1)} %get-tuple-element.11), channel_id=1, source_target_pairs={{0,16},{4,20},{8,24},{12,28},{1,17},{5,21},{9,25},{13,29},{2,18},{... | collective-permute-start | bytes 786440 | tf_op jit(solution)/shard_map/ppermute | solution.py:18
  29.2 16.5 %copy-start.16 = (s32[1,16]{1,0:T(1,128)S(1)}, s32[1,16]{1,0:T(1,128)}, u32[]{:S(2)}) copy-start(s32[1,16]{1,0:T(1,128)} %param.6) | copy-start | bytes 196
  29.2 12.0 %collective-permute-start.3 = (bf16[2,20,2,16,128]{4,3,2,1,0:T(8,128)(2,1)S(1)}, bf16[2,20,2,16,128]{4,3,2,1,0:T(8,128)(2,1)S(1)}, u32[]{:S(2)}, u32[]{:S(2)}) collective-permute-start(bf16[2,20,2,16,128]{4,3,2,1,0:T(8,128)(2,1)S(1)} %get-tuple-element.10), channel_id=1, source_target_pairs={{8,0},{12,4},{16,8},{20,12},{24,16},{28,20},{9,1},{13,5},{17,9},{2... | collective-permute-start | bytes 983048 | tf_op jit(solution)/shard_map/ppermute | solution.py:18
  30.6 11.9 %collective-permute-start.2 = (bf16[2,20,2,16,128]{4,3,2,1,0:T(8,128)(2,1)S(1)}, bf16[2,20,2,16,128]{4,3,2,1,0:T(8,128)(2,1)S(1)}, u32[]{:S(2)}, u32[]{:S(2)}) collective-permute-start(bf16[2,20,2,16,128]{4,3,2,1,0:T(8,128)(2,1)S(1)} %get-tuple-element.9), channel_id=1, source_target_pairs={{0,8},{4,12},{8,16},{12,20},{16,24},{20,28},{1,9},{5,13},{9,17},{1... | collective-permute-start | bytes 983048 | tf_op jit(solution)/shard_map/ppermute | solution.py:18
  35.6 41.8 %copy-start.11 = (bf16[3,3,1,128,128]{4,3,2,1,0:T(8,128)(2,1)}, bf16[3,3,1,128,128]{4,3,2,1,0:T(8,128)(2,1)S(1)}, u32[]{:S(2)}) copy-start(bf16[3,3,1,128,128]{4,3,2,1,0:T(8,128)(2,1)S(1)} %get-tuple-element.19) | copy-start | bytes 884740
  35.6 41.8 %copy-start.12 = (bf16[3,3,1,128,128]{4,3,2,1,0:T(8,128)(2,1)}, bf16[3,3,1,128,128]{4,3,2,1,0:T(8,128)(2,1)S(1)}, u32[]{:S(2)}) copy-start(bf16[3,3,1,128,128]{4,3,2,1,0:T(8,128)(2,1)S(1)} %get-tuple-element.20) | copy-start | bytes 884740
  35.6 41.8 %copy-start.13 = (bf16[3,3,1,128,128]{4,3,2,1,0:T(8,128)(2,1)}, bf16[3,3,1,128,128]{4,3,2,1,0:T(8,128)(2,1)S(1)}, u32[]{:S(2)}) copy-start(bf16[3,3,1,128,128]{4,3,2,1,0:T(8,128)(2,1)S(1)} %get-tuple-element.21) | copy-start | bytes 884740
  44.4 12.9 %collective-permute-start.5 = (bf16[2,20,20,1,128]{4,3,2,1,0:T(2,128)(2,1)S(1)}, bf16[2,20,20,1,128]{4,3,2,1,0:T(2,128)(2,1)S(1)}, u32[]{:S(2)}, u32[]{:S(2)}) collective-permute-start(bf16[2,20,20,1,128]{4,3,2,1,0:T(2,128)(2,1)S(1)} %get-tuple-element.8), channel_id=1, source_target_pairs={{4,0},{8,4},{12,8},{16,12},{20,16},{24,20},{28,24},{5,1},{9,5},{13... | collective-permute-start | bytes 614408 | tf_op jit(solution)/shard_map/ppermute | solution.py:18
  46.2 20.0 %collective-permute-start.4 = (bf16[2,20,20,1,128]{4,3,2,1,0:T(2,128)(2,1)S(1)}, bf16[2,20,20,1,128]{4,3,2,1,0:T(2,128)(2,1)S(1)}, u32[]{:S(2)}, u32[]{:S(2)}) collective-permute-start(bf16[2,20,20,1,128]{4,3,2,1,0:T(2,128)(2,1)S(1)} %get-tuple-element.7), channel_id=1, source_target_pairs={{0,4},{4,8},{8,12},{12,16},{16,20},{20,24},{24,28},{1,5},{5,9},{9,... | collective-permute-start | bytes 614408 | tf_op jit(solution)/shard_map/ppermute | solution.py:18
  72.5 3.0 %copy-start = (bf16[2,20,20,18,128]{4,3,2,1,0:T(8,128)(2,1)}, bf16[2,20,20,18,128]{4,3,2,1,0:T(8,128)(2,1)S(1)}, u32[]{:S(2)}) copy-start(bf16[2,20,20,18,128]{4,3,2,1,0:T(8,128)(2,1)S(1)} %pad_maximum_fusion) | copy-start | bytes 11059204
  105.7 4.5 %copy-start.1 = (f32[18,18,1,24,128]{4,3,1,0,2:T(8,128)S(1)}, f32[18,18,1,24,128]{4,3,1,0,2:T(8,128)}, u32[]{:S(2)}) copy-start(f32[18,18,1,24,128]{4,3,1,0,2:T(8,128)} %reshape.72) | copy-start | bytes 11943940
  113.2 3.9 %copy-start.9 = (f32[18,18,8,3,128]{4,2,3,1,0:T(8,128)S(1)}, f32[18,18,8,3,128]{4,2,3,1,0:T(8,128)}, u32[]{:S(2)}) copy-start(f32[18,18,8,3,128]{4,2,3,1,0:T(8,128)} %get-tuple-element.26) | copy-start | bytes 11943940
  138.7 3.2 %copy-start.5 = (bf16[20,20,20,128]{3,2,1,0:T(8,128)(2,1)S(1)}, bf16[20,20,20,128]{3,2,1,0:T(8,128)(2,1)}, u32[]{:S(2)}) copy-start(bf16[20,20,20,128]{3,2,1,0:T(8,128)(2,1)} %get-tuple-element.5) | copy-start | bytes 6144004
  138.7 4.3 %copy-start.3 = (f32[18,18,18,128]{3,2,1,0:T(8,128)S(1)}, f32[18,18,18,128]{3,2,1,0:T(8,128)}, u32[]{:S(2)}) copy-start(f32[18,18,18,128]{3,2,1,0:T(8,128)} %add_divide_fusion) | copy-start | bytes 8957956
  140.3 3.8 %copy-start.2 = (f32[18,18,18,128]{3,2,1,0:T(8,128)S(1)}, f32[18,18,18,128]{3,2,1,0:T(8,128)}, u32[]{:S(2)}) copy-start(f32[18,18,18,128]{3,2,1,0:T(8,128)} %slice_bitcast_fusion.1) | copy-start | bytes 8957956
  180.7 1.9 copy-start.7
  180.7 2.2 copy-start.10
  180.7 2.2 copy-start.17
  182.0 100.2 %all-reduce.7.cloned.1.call-start = ((), (), s32[]{:S(2)}) async-start(), calls=%async_computation.2 | async-start | bytes 442368 | tf_op jit(solution)/shard_map/psum | solution.py:166
  197.0 11.1 %copy-start.8 = (bf16[1,16,8,8,512]{4,3,2,1,0:T(8,128)(2,1)S(1)}, bf16[1,16,8,8,512]{4,3,2,1,0:T(8,128)(2,1)}, u32[]{:S(2)}) copy-start(bf16[1,16,8,8,512]{4,3,2,1,0:T(8,128)(2,1)} %param.4) | copy-start | bytes 3145732
  197.0 11.1 %copy-start.15 = (f32[16]{0:T(128)S(1)}, f32[16]{0:T(128)}, u32[]{:S(2)}) copy-start(f32[16]{0:T(128)} %convert_bitcast_fusion.1) | copy-start | bytes 196
  (3 other events, 3.7 us)
Sparse Core Ops, SparseCore 0:
  182.2 25.7 reduce-scatter.1
  211.4 70.8 all-reduce.6
where the time goes:
time: 296 us; the launch traced here: 291 us
  waiting for transfers between devices  101 us (34%)
  matrix products  62.5 us (21%)
  local copies, waits for them, and re-layouts  51 us (17%)
  other arithmetic  33.8 us (11%)
  starting transfers between devices  20.3 us (7%)
  between operations  14.9 us (5%)
  blocking collectives  7.7 us (3%)
    psum x1, waiting for transfers between devices, local(): grad_part = lax.psum(grad_part, 'space')  70 us
    transpose x1, matrix products, kernel_grad(): return out.transpose(1, 2, 3, 0, 4)  32.2 us
    conv_general_dilated x2, matrix products, conv(): lax.conv_general_dilated(volume[None], kernel, (1, 1, 1), 'VALID', dimens...  30.3 us
    ppermute x6, waiting for transfers between devices, from_behind(): return lax.ppermute(shard, axis, pairs)  23.2 us
    conv_general_dilated x9, local copies, waits for them, and re-layouts, conv(): lax.conv_general_dilated(volume[None], kernel, (1, 1, 1), 'VALID', dimens...  20.1 us
    ppermute x6, starting transfers between devices, from_behind(): return lax.ppermute(shard, axis, pairs)  20 us
    mul x2, local copies, waits for them, and re-layouts, local(): slope_ext = gate_ext * (1.0 + pre_ext * (1.0 - gate_ext))  11.3 us
    all_gather x1, blocking collectives, local(): weight_full = lax.all_gather(weight, 'fsdp', axis=1, tiled=True)  7.7 us
  transfers between devices with their start and end apart: 8, of which 7 were waited for; matrix products, arithmetic and copies ran while one was open for 8% of the time, Pallas kernels for 0%

commit v1 on v0

--- a/solution.py
+++ b/solution.py
@@ -163,7 +163,8 @@
     grad_sup = kernel_grad(padded_in[1:-1, 1:-1, 1:-1], grad_ext[1:-1, 1:-1, 1:-1])
     grad_term = fold_kernel_grad(grad_sup, channels) / math.sqrt(total_cells)
     grad_part = lax.psum_scatter(grad_term, "fsdp", scatter_dimension=1, tiled=True)
-    grad_part = lax.psum(grad_part, "space")
+    return_all_forms_on = lambda own_rows, axis_key: lax.all_gather(own_rows, axis_key).sum(axis=0)
+    grad_part = return_all_forms_on(grad_part, "space")
     return (activations[None], input_grad[None], grad_part)
 
 

time: 296 us -> 257 us (0.87)
  waiting for transfers between devices: 101 us -> 29.6 us
  blocking collectives: 7.7 us -> 47.2 us
  local copies, waits for them, and re-layouts: 51 us -> 45.1 us
    psum x1 -> x0, waiting for transfers between devices: 70 us -> none  [local(): grad_part = lax.psum(grad_part, 'space')]
    all_gather x0 -> x1, blocking collectives: none -> 39.5 us  [local(): lax.all_gather(own_rows, axis_key).sum(axis=0)]
    unnamed x40 -> x41, local copies, waits for them, and re-layouts: 6.21 us -> 3.55 us
  transfers between devices with their start and end apart: 8 -> 7, of which waited for: 7 -> 6; matrix products, arithmetic and copies ran while one was open for 8% -> 8% of each run, Pallas kernels for 0% -> 0%
where the time goes in v1:
time: 257 us; the launch traced here: 253 us
  matrix products  63 us (25%)
  blocking collectives  47.2 us (18%)
  local copies, waits for them, and re-layouts  45.1 us (18%)
  other arithmetic  32.7 us (13%)
  waiting for transfers between devices  29.6 us (12%)
  starting transfers between devices  20.1 us (8%)
  between operations  14.9 us (6%)
    all_gather x1, blocking collectives, local(): lax.all_gather(own_rows, axis_key).sum(axis=0)  39.5 us
    transpose x1, matrix products, kernel_grad(): return out.transpose(1, 2, 3, 0, 4)  32.2 us
    conv_general_dilated x2, matrix products, conv(): lax.conv_general_dilated(volume[None], kernel, (1, 1, 1), 'VALID', dimens...  30.8 us
    ppermute x6, waiting for transfers between devices, from_behind(): return lax.ppermute(shard, axis, pairs)  23.2 us
    ppermute x6, starting transfers between devices, from_behind(): return lax.ppermute(shard, axis, pairs)  20 us
    conv_general_dilated x9, local copies, waits for them, and re-layouts, conv(): lax.conv_general_dilated(volume[None], kernel, (1, 1, 1), 'VALID', dimens...  19.5 us
    mul x2, local copies, waits for them, and re-layouts, local(): slope_ext = gate_ext * (1.0 + pre_ext * (1.0 - gate_ext))  11.3 us
    all_gather x1, blocking collectives, local(): weight_full = lax.all_gather(weight, 'fsdp', axis=1, tiled=True)  7.7 us
  transfers between devices with their start and end apart: 7, of which 6 were waited for; matrix products, arithmetic and copies ran while one was open for 8% of the time, Pallas kernels for 0%

profile of v1, /device:TPU:0, one launch (start us, length us, event | category | flops | bytes accessed | tf_op | source)
XLA Modules:
  0.0 252.6 jit_solution(14823312713849300885)
XLA Ops:
  12.0 6.7 %collective-permute-start = (bf16[2,2,16,16,128]{4,3,2,1,0:T(8,128)(2,1)S(1)}, bf16[2,2,16,16,128]{4,3,2,1,0:T(8,128)(2,1)S(1)}, u32[]{:S(2)}, u32[]{:S(2)}) collective-permute-start(bf16[2,2,16,16,128]{4,3,2,1,0:T(8,128)(2,1)S(1)} %get-tuple-element.11), channel_id=1, source_target_pairs={{0,16},{4,20},{8,24},{12,28},{1,17},{5,21},{9,25},{13,29},{2,18},{... | collective-permute-start | bytes 786440 | tf_op jit(solution)/shard_map/ppermute | solution.py:18
  18.7 7.7 %all_gather.9 = bf16[27,64,64]{2,1,0:T(8,128)(2,1)S(1)} all-gather(bf16[27,16,64]{2,1,0:T(8,128)(2,1)S(1)} %copy-done.15), channel_id=1, replica_groups=mesh['space'=8,'fsdp'=4] {'fsdp'}, dimensions={1}, use_global_device_ids=true | all-gather | bytes 276480 | tf_op jit(solution)/shard_map/all_gather | solution.py:135
  30.6 4.8 %collective-permute-start.2 = (bf16[2,20,2,16,128]{4,3,2,1,0:T(8,128)(2,1)S(1)}, bf16[2,20,2,16,128]{4,3,2,1,0:T(8,128)(2,1)S(1)}, u32[]{:S(2)}, u32[]{:S(2)}) collective-permute-start(bf16[2,20,2,16,128]{4,3,2,1,0:T(8,128)(2,1)S(1)} %get-tuple-element.9), channel_id=1, source_target_pairs={{0,8},{4,12},{8,16},{12,20},{16,24},{20,28},{1,9},{5,13},{9,17},{1... | collective-permute-start | bytes 983048 | tf_op jit(solution)/shard_map/ppermute | solution.py:18
  35.7 5.6 %collective-permute-done.3 = bf16[2,20,2,16,128]{4,3,2,1,0:T(8,128)(2,1)S(1)} collective-permute-done((bf16[2,20,2,16,128]{4,3,2,1,0:T(8,128)(2,1)S(1)}, bf16[2,20,2,16,128]{4,3,2,1,0:T(8,128)(2,1)S(1)}, u32[]{:S(2)}, u32[]{:S(2)}) %collective-permute-start.3) | collective-permute-done | bytes 327712 | tf_op jit(solution)/shard_map/ppermute | solution.py:18
  46.2 4.7 %collective-permute-start.4 = (bf16[2,20,20,1,128]{4,3,2,1,0:T(2,128)(2,1)S(1)}, bf16[2,20,20,1,128]{4,3,2,1,0:T(2,128)(2,1)S(1)}, u32[]{:S(2)}, u32[]{:S(2)}) collective-permute-start(bf16[2,20,20,1,128]{4,3,2,1,0:T(2,128)(2,1)S(1)} %get-tuple-element.7), channel_id=1, source_target_pairs={{0,4},{4,8},{8,12},{12,16},{16,20},{20,24},{24,28},{1,5},{5,9},{9,... | collective-permute-start | bytes 614408 | tf_op jit(solution)/shard_map/ppermute | solution.py:18
  50.9 6.3 %collective-permute-done.5 = bf16[2,20,20,1,128]{4,3,2,1,0:T(2,128)(2,1)S(1)} collective-permute-done((bf16[2,20,20,1,128]{4,3,2,1,0:T(2,128)(2,1)S(1)}, bf16[2,20,20,1,128]{4,3,2,1,0:T(2,128)(2,1)S(1)}, u32[]{:S(2)}, u32[]{:S(2)}) %collective-permute-start.5) | collective-permute-done | bytes 204832 | tf_op jit(solution)/shard_map/ppermute | solution.py:18
  57.7 8.5 %collective-permute-done.4 = bf16[2,20,20,1,128]{4,3,2,1,0:T(2,128)(2,1)S(1)} collective-permute-done((bf16[2,20,20,1,128]{4,3,2,1,0:T(2,128)(2,1)S(1)}, bf16[2,20,20,1,128]{4,3,2,1,0:T(2,128)(2,1)S(1)}, u32[]{:S(2)}, u32[]{:S(2)}) %collective-permute-start.4) | collective-permute-done | bytes 204832 | tf_op jit(solution)/shard_map/ppermute | solution.py:18
  66.6 5.9 %pad_maximum_fusion = bf16[2,20,20,18,128]{4,3,2,1,0:T(8,128)(2,1)S(1)} fusion(bf16[2,20,20,1,128]{4,3,2,1,0:T(2,128)(2,1)S(1)} %broadcast_select_fusion.1, bf16[2,20,2,16,128]{4,3,2,1,0:T(8,128)(2,1)S(1)} %broadcast_select_fusion.3, bf16[2,2,16,16,128]{4,3,2,1,0:T(8,128)(2,1)S(1)} %broadcast_select_fusion.5, bf16[1,16,16,16,128]{4,3,2,1,0:T(8,128)(2,1)S(1)} %bitcast.90, ...), kind=kLoop, calls=%fused_computation.6 | loop fusion | flops 29491200 | bytes 7372800 | tf_op jit(solution)/shard_map/concatenate | solution.py:63
  72.5 3.0 %fusion.29 = (bf16[20,20,20,128]{3,2,1,0:T(8,128)(2,1)}, bf16[20,20,1,20,128]{4,3,1,0,2:T(8,128)(2,1)S(1)}) fusion(bf16[2,20,20,18,128]{4,3,2,1,0:T(8,128)(2,1)S(1)} %pad_maximum_fusion), kind=kLoop, calls=%fused_computation.39 | loop fusion | bytes 7782400 | tf_op jit(solution)/shard_map/squeeze | solution.py:148
  77.5 17.2 %add_multiply_fusion = (f32[18,18,8,3,128]{4,2,3,1,0:T(8,128)}, f32[18,18,8,3,128]{4,2,3,1,0:T(8,128)S(1)}) fusion(bf16[3,3,1,128,128]{4,3,2,1,0:T(8,128)(2,1)S(1)} %get-tuple-element.21, bf16[3,3,1,128,128]{4,3,2,1,0:T(8,128)(2,1)S(1)} %get-tuple-element.20, bf16[3,3,1,128,128]{4,3,2,1,0:T(8,128)(2,1)S(1)} %get-tuple-element.19, ...), kind=kOutput, calls=%fused_computation.17 | convolution fusion | flops 6900842496 | bytes 12738584 | tf_op jit(solution)/shard_map/conv_general_dilated | solution.py:102
  94.7 4.0 %copy.59 = f32[18,18,8,3,128]{4,3,2,1,0:T(4,128)} copy(f32[18,18,8,3,128]{4,2,3,1,0:T(8,128)S(1)} %get-tuple-element.27) | data formatting | bytes 7962624 | tf_op jit(solution)/shard_map/conv_general_dilated | solution.py:102
  98.6 7.3 %reshape.72 = f32[18,18,1,24,128]{4,3,1,0,2:T(8,128)} reshape(f32[18,18,8,3,128]{4,3,2,1,0:T(4,128)} %copy.59) | data formatting | bytes 7962624 | tf_op jit(solution)/shard_map/conv_general_dilated | solution.py:102
  105.9 4.5 %slice_bitcast_fusion.1 = f32[18,18,18,128]{3,2,1,0:T(8,128)} fusion(f32[18,18,1,24,128]{4,3,1,0,2:T(8,128)} %reshape.72), kind=kLoop, calls=%fused_computation.16 | loop fusion | bytes 5971968 | tf_op jit(solution)/shard_map/squeeze | solution.py:102
  110.5 3.0 %add_divide_fusion = f32[18,18,18,128]{3,2,1,0:T(8,128)} fusion(f32[18,18,1,24,128]{4,3,1,0,2:T(8,128)S(1)} %copy-done.1), kind=kLoop, calls=%fused_computation.18 | loop fusion | flops 2239488 | bytes 5971968 | tf_op jit(solution)/shard_map/div | solution.py:151
  113.5 3.9 %convert_bitcast_fusion = f32[18,18,18,128]{3,2,1,0:T(8,128)} fusion(bf16[2,20,20,18,128]{4,3,2,1,0:T(8,128)(2,1)} %copy-done), kind=kLoop, calls=%fused_computation.4 | loop fusion | flops 746496 | bytes 4478976 | tf_op jit(solution)/shard_map/convert_element_type | solution.py:153
  117.3 4.0 %copy.61 = f32[18,18,8,3,128]{4,3,2,1,0:T(4,128)} copy(f32[18,18,8,3,128]{4,2,3,1,0:T(8,128)S(1)} %copy-done.10) | data formatting | bytes 7962624 | tf_op jit(solution)/shard_map/mul | solution.py:152
  121.3 7.3 %reshape.81 = f32[18,18,1,24,128]{4,3,1,0,2:T(8,128)} reshape(f32[18,18,8,3,128]{4,3,2,1,0:T(4,128)} %copy.61) | data formatting | bytes 7962624 | tf_op jit(solution)/shard_map/mul | solution.py:152
  128.6 3.2 %fusion.22 = bf16[18,18,1,18,128]{4,3,1,0,2:T(8,128)(2,1)S(1)} fusion(f32[18,18,1,24,128]{4,3,1,0,2:T(8,128)} %reshape.81, bf16[2,20,20,18,128]{4,3,2,1,0:T(8,128)(2,1)} %copy-done), kind=kLoop, calls=%fused_computation.33 | loop fusion | flops 2239488 | bytes 5971968 | tf_op jit(solution)/shard_map/convert_element_type | solution.py:153
  132.1 2.9 %reshape.75 = bf16[18,18,1,8,3,128]{5,4,3,1,0,2:T(4,128)(2,1)} reshape(bf16[18,18,1,24,128]{4,3,1,0,2:T(8,128)(2,1)S(1)} %pad.11) | data formatting | bytes 3981312 | tf_op jit(solution)/shard_map/conv_general_dilated | solution.py:102
  141.2 4.3 %fusion.31 = (bf16[1,16,16,16,128]{4,3,2,1,0:T(8,128)(2,1)S(1)}, f32[16,16,16,128]{3,2,1,0:T(8,128)}) fusion(f32[18,18,18,128]{3,2,1,0:T(8,128)S(1)} %copy-done.2, f32[18,18,18,128]{3,2,1,0:T(8,128)S(1)} %copy-done.3, f32[18,18,18,128]{3,2,1,0:T(8,128)} %convert_bitcast_fusion), kind=kLoop, calls=%fused_computation.41 | loop fusion | flops 3670016 | bytes 9437184 | tf_op jit(solution)/shard_map/broadcast_in_dim | solution.py:115
  145.5 32.2 %fusion.17 = f32[3,3,3,128,128]{4,3,2,1,0:T(8,128)S(1)} fusion(bf16[1,18,18,18,128]{4,3,2,1,0:T(8,128)(2,1)S(1)} %slice_bitcast_fusion.2, bf16[1,16,16,16,128]{4,3,2,1,0:T(8,128)(2,1)S(1)} %get-tuple-element.3), kind=kOutput, calls=%fused_computation.25 | convolution fusion | flops 3623878656 | bytes 4311040 | tf_op jit(solution)/shard_map/transpose | solution.py:121
  179.9 13.6 %fusion.25 = f32[16,16,8,3,128]{4,2,3,1,0:T(8,128)S(1)} fusion(bf16[18,18,1,7,2,128]{5,3,4,1,0,2:T(8,128)(2,1)S(1)} %copy-done.11, bf16[18,18,1,8,3,128]{5,3,4,1,0,2:T(8,128)(2,1)S(1)} %copy-done.7, pred[8,3]{0,1:T(4,128)(4,1)S(1)} %copy-done.18, bf16[3,3,1,128,128]{4,3,2,1,0:T(8,128)(2,1)} %copy-done.14, bf16[3,3,1,128,128]{4,3,2,1,0:T(8,128)(2,1)} %copy-done.13, ...), kind=kOutput, calls=%fused_computation.37 | convolution fusion | flops 5447442432 | bytes 7182360 | tf_op jit(solution)/shard_map/conv_general_dilated | solution.py:102
  198.7 6.4 %reduce-scatter.2.cloned.1.call-done = f32[27,16,64]{2,1,0:T(8,128)} async-done(((f32[27,64,64]{2,1,0:T(8,128)}), f32[27,16,64]{2,1,0:T(8,128)}) %reduce-scatter.2.cloned.1.call-update) | async-done | bytes 110608 | tf_op jit(solution)/shard_map/reduce_scatter | solution.py:165
  205.0 39.5 %all-gather = f32[216,16,64]{2,1,0:T(8,128)S(1)} all-gather(f32[27,16,64]{2,1,0:T(8,128)} %reduce-scatter.2.cloned.1.call-done), channel_id=2, replica_groups=mesh['space'=8,'fsdp'=4] {'space'}, dimensions={0}, use_global_device_ids=true | all-gather | bytes 995328 | tf_op jit(solution)/shard_map/all_gather | solution.py:166
  (79 shorter events, 31.5 us)
Async XLA Ops:
  7.2 11.5 %copy-start.15 = (bf16[27,16,64]{2,1,0:T(8,128)(2,1)S(1)}, bf16[27,16,64]{2,1,0:T(8,128)(2,1)}, u32[]{:S(2)}) copy-start(bf16[27,16,64]{2,1,0:T(8,128)(2,1)} %param.7) | copy-start | bytes 165892
  7.2 197.9 %reduce-scatter.2.cloned.1.call-start = ((), (), s32[]{:S(2)}) async-start(), calls=%async_computation.1 | async-start | bytes 1105920 | tf_op jit(solution)/shard_map/reduce_scatter | solution.py:165
  10.7 17.4 %collective-permute-start.1 = (bf16[2,2,16,16,128]{4,3,2,1,0:T(8,128)(2,1)S(1)}, bf16[2,2,16,16,128]{4,3,2,1,0:T(8,128)(2,1)}, u32[]{:S(2)}, u32[]{:S(2)}) collective-permute-start(bf16[2,2,16,16,128]{4,3,2,1,0:T(8,128)(2,1)S(1)} %get-tuple-element.12), channel_id=1, source_target_pairs={{16,0},{20,4},{24,8},{28,12},{17,1},{21,5},{25,9},{29,13},{18,2},{... | collective-permute-start | bytes 786440 | tf_op jit(solution)/shard_map/ppermute | solution.py:18
  12.0 17.0 %collective-permute-start = (bf16[2,2,16,16,128]{4,3,2,1,0:T(8,128)(2,1)S(1)}, bf16[2,2,16,16,128]{4,3,2,1,0:T(8,128)(2,1)S(1)}, u32[]{:S(2)}, u32[]{:S(2)}) collective-permute-start(bf16[2,2,16,16,128]{4,3,2,1,0:T(8,128)(2,1)S(1)} %get-tuple-element.11), channel_id=1, source_target_pairs={{0,16},{4,20},{8,24},{12,28},{1,17},{5,21},{9,25},{13,29},{2,18},{... | collective-permute-start | bytes 786440 | tf_op jit(solution)/shard_map/ppermute | solution.py:18
  29.2 16.5 %copy-start.17 = (s32[1,16]{1,0:T(1,128)S(1)}, s32[1,16]{1,0:T(1,128)}, u32[]{:S(2)}) copy-start(s32[1,16]{1,0:T(1,128)} %param.6) | copy-start | bytes 196
  29.2 12.0 %collective-permute-start.3 = (bf16[2,20,2,16,128]{4,3,2,1,0:T(8,128)(2,1)S(1)}, bf16[2,20,2,16,128]{4,3,2,1,0:T(8,128)(2,1)S(1)}, u32[]{:S(2)}, u32[]{:S(2)}) collective-permute-start(bf16[2,20,2,16,128]{4,3,2,1,0:T(8,128)(2,1)S(1)} %get-tuple-element.10), channel_id=1, source_target_pairs={{8,0},{12,4},{16,8},{20,12},{24,16},{28,20},{9,1},{13,5},{17,9},{2... | collective-permute-start | bytes 983048 | tf_op jit(solution)/shard_map/ppermute | solution.py:18
  30.6 11.9 %collective-permute-start.2 = (bf16[2,20,2,16,128]{4,3,2,1,0:T(8,128)(2,1)S(1)}, bf16[2,20,2,16,128]{4,3,2,1,0:T(8,128)(2,1)S(1)}, u32[]{:S(2)}, u32[]{:S(2)}) collective-permute-start(bf16[2,20,2,16,128]{4,3,2,1,0:T(8,128)(2,1)S(1)} %get-tuple-element.9), channel_id=1, source_target_pairs={{0,8},{4,12},{8,16},{12,20},{16,24},{20,28},{1,9},{5,13},{9,17},{1... | collective-permute-start | bytes 983048 | tf_op jit(solution)/shard_map/ppermute | solution.py:18
  35.6 41.8 %copy-start.12 = (bf16[3,3,1,128,128]{4,3,2,1,0:T(8,128)(2,1)}, bf16[3,3,1,128,128]{4,3,2,1,0:T(8,128)(2,1)S(1)}, u32[]{:S(2)}) copy-start(bf16[3,3,1,128,128]{4,3,2,1,0:T(8,128)(2,1)S(1)} %get-tuple-element.19) | copy-start | bytes 884740
  35.6 41.8 %copy-start.13 = (bf16[3,3,1,128,128]{4,3,2,1,0:T(8,128)(2,1)}, bf16[3,3,1,128,128]{4,3,2,1,0:T(8,128)(2,1)S(1)}, u32[]{:S(2)}) copy-start(bf16[3,3,1,128,128]{4,3,2,1,0:T(8,128)(2,1)S(1)} %get-tuple-element.20) | copy-start | bytes 884740
  35.7 41.8 %copy-start.14 = (bf16[3,3,1,128,128]{4,3,2,1,0:T(8,128)(2,1)}, bf16[3,3,1,128,128]{4,3,2,1,0:T(8,128)(2,1)S(1)}, u32[]{:S(2)}) copy-start(bf16[3,3,1,128,128]{4,3,2,1,0:T(8,128)(2,1)S(1)} %get-tuple-element.21) | copy-start | bytes 884740
  44.4 12.9 %collective-permute-start.5 = (bf16[2,20,20,1,128]{4,3,2,1,0:T(2,128)(2,1)S(1)}, bf16[2,20,20,1,128]{4,3,2,1,0:T(2,128)(2,1)S(1)}, u32[]{:S(2)}, u32[]{:S(2)}) collective-permute-start(bf16[2,20,20,1,128]{4,3,2,1,0:T(2,128)(2,1)S(1)} %get-tuple-element.8), channel_id=1, source_target_pairs={{4,0},{8,4},{12,8},{16,12},{20,16},{24,20},{28,24},{5,1},{9,5},{13... | collective-permute-start | bytes 614408 | tf_op jit(solution)/shard_map/ppermute | solution.py:18
  46.2 20.0 %collective-permute-start.4 = (bf16[2,20,20,1,128]{4,3,2,1,0:T(2,128)(2,1)S(1)}, bf16[2,20,20,1,128]{4,3,2,1,0:T(2,128)(2,1)S(1)}, u32[]{:S(2)}, u32[]{:S(2)}) collective-permute-start(bf16[2,20,20,1,128]{4,3,2,1,0:T(2,128)(2,1)S(1)} %get-tuple-element.7), channel_id=1, source_target_pairs={{0,4},{4,8},{8,12},{12,16},{16,20},{20,24},{24,28},{1,5},{5,9},{9,... | collective-permute-start | bytes 614408 | tf_op jit(solution)/shard_map/ppermute | solution.py:18
  72.5 3.0 %copy-start = (bf16[2,20,20,18,128]{4,3,2,1,0:T(8,128)(2,1)}, bf16[2,20,20,18,128]{4,3,2,1,0:T(8,128)(2,1)S(1)}, u32[]{:S(2)}) copy-start(bf16[2,20,20,18,128]{4,3,2,1,0:T(8,128)(2,1)S(1)} %pad_maximum_fusion) | copy-start | bytes 11059204
  105.9 4.5 %copy-start.1 = (f32[18,18,1,24,128]{4,3,1,0,2:T(8,128)S(1)}, f32[18,18,1,24,128]{4,3,1,0,2:T(8,128)}, u32[]{:S(2)}) copy-start(f32[18,18,1,24,128]{4,3,1,0,2:T(8,128)} %reshape.72) | copy-start | bytes 11943940
  113.4 3.9 %copy-start.10 = (f32[18,18,8,3,128]{4,2,3,1,0:T(8,128)S(1)}, f32[18,18,8,3,128]{4,2,3,1,0:T(8,128)}, u32[]{:S(2)}) copy-start(f32[18,18,8,3,128]{4,2,3,1,0:T(8,128)} %get-tuple-element.26) | copy-start | bytes 11943940
  135.1 3.8 %copy-start.5 = (bf16[20,20,20,128]{3,2,1,0:T(8,128)(2,1)S(1)}, bf16[20,20,20,128]{3,2,1,0:T(8,128)(2,1)}, u32[]{:S(2)}) copy-start(bf16[20,20,20,128]{3,2,1,0:T(8,128)(2,1)} %get-tuple-element.5) | copy-start | bytes 6144004
  135.1 4.9 %copy-start.3 = (f32[18,18,18,128]{3,2,1,0:T(8,128)S(1)}, f32[18,18,18,128]{3,2,1,0:T(8,128)}, u32[]{:S(2)}) copy-start(f32[18,18,18,128]{3,2,1,0:T(8,128)} %add_divide_fusion) | copy-start | bytes 8957956
  137.3 8.1 %copy-start.6 = (bf16[18,18,1,8,3,128]{5,3,4,1,0,2:T(8,128)(2,1)}, bf16[18,18,1,8,3,128]{5,3,4,1,0,2:T(8,128)(2,1)S(1)}, u32[]{:S(2)}) copy-start(bf16[18,18,1,8,3,128]{5,3,4,1,0,2:T(8,128)(2,1)S(1)} %copy.63) | copy-start | bytes 5971972
  137.4 3.8 %copy-start.2 = (f32[18,18,18,128]{3,2,1,0:T(8,128)S(1)}, f32[18,18,18,128]{3,2,1,0:T(8,128)}, u32[]{:S(2)}) copy-start(f32[18,18,18,128]{3,2,1,0:T(8,128)} %slice_bitcast_fusion.1) | copy-start | bytes 8957956
  177.7 2.2 copy-start.11
  177.7 2.2 copy-start.18
  194.3 2.0 copy-start.8
  194.3 2.0 copy-start.9
  194.3 2.0 copy-start.16
  (3 other events, 4.3 us)
Sparse Core Ops, SparseCore 0:
  179.2 25.7 reduce-scatter.1
